TPU v7x, 512 devices: a whole 4x4x16 slice. The times are simulated.
512 devices in a mesh: seq: 64 (over y, z_lo, core), tp: 8 (over z_hi, x).
Axes of the slice: x: 4, y: 4, z: 16 (z_hi: 2, z_lo: 8; z = z_hi * 8 + z_lo), core: 2. Of those that a mesh axis runs over, the one named last changes fastest.
Arguments:
- tokens: bfloat16 [16384, 4096], P('seq', 'tp'), may hold values from -6 to 6
- ln_gain: float32 [4096], replicated, may hold values from 0.1 to 1.9
- ln_bias: float32 [4096], replicated, may hold values from -3 to 3
- w_qkv: bfloat16 [4096, 16, 3, 128], P('seq', 'tp'), may hold values from -3 to 3
- w_out: bfloat16 [16, 128, 4096], P('tp', None, 'seq'), may hold values from -0.25 to 0.25
- layer_scale: float32 [4096], P('tp'), may hold values from 0.5 to 2
- grids: int32 [14], replicated, may hold values from 24 to 40, as said below
- offsets: int32 [15], replicated, may hold values from 0 to 15302, as said below
Outputs:
- merged: bfloat16 [16384, 4, 4096], P('seq', None, 'tp')
Inputs may be any that keep to these rules, and one draw needn't show every extreme that they name: `grids`: every side is even and some image has side exactly 40. Of images 2k and 2k + 1, one side is drawn and the other is the largest even side of at most 40 whose square keeps the two squares' sum within 2176. offsets[0] = 0 and offsets[s + 1] = offsets[s] + 5 + grids[s] * grids[s].
All inputs are finite; a program needn't handle non-finite values.
Results may differ from a plain program's by a relative error of at most 0.015.
Values may be sent and summed in bfloat16 or wider, within the bound.
No kernel may reach another device: no remote copies, remote signals or barrier semaphores. Data moves between devices by JAX's collectives and lax.ppermute only.
A program may use at most 64 MiB of HBM per device.

v0:
```python
import math
import jax
import jax.numpy as jnp
from jax import lax
from jax.sharding import PartitionSpec as P

HALO = 48
REACH = 7


def from_behind(shard, axis, by):
    count = lax.axis_size(axis)
    pairs = [(i, i + by) for i in range(count) if 0 <= i + by < count]
    return lax.ppermute(shard, axis, pairs)


def layout_rows(row_ids, offsets, grids, row_count):
    images = grids.shape[0]
    image_ends = offsets[1:]
    segment = jnp.sum((row_ids[:, None] >= image_ends[None, :]).astype(jnp.int32), axis=1)
    inside = (row_ids >= 0) & (row_ids < row_count) & (segment < images)
    onehot = (
        jnp.minimum(segment, images - 1)[:, None] == jnp.arange(images, dtype=jnp.int32)[None, :]
    ).astype(jnp.int32)
    image_start = jnp.sum(onehot * offsets[None, :-1], axis=1)
    grid_side = jnp.sum(onehot * grids[None, :], axis=1)
    position = row_ids - image_start
    is_patch = inside & (position >= 5)
    patch_index = jnp.maximum(position - 5, 0)
    return (segment, inside, is_patch, patch_index // grid_side, patch_index % grid_side, grid_side)


def rotate(vectors, is_patch, grid_row, grid_col, grid_side):
    quarter = vectors.shape[-1] // 4
    frequency = 2.0 * math.pi * jnp.power(100.0, -jnp.arange(quarter, dtype=jnp.float32) / quarter)
    side_float = grid_side.astype(jnp.float32)
    coord_row = (2 * grid_row + 1).astype(jnp.float32) / side_float - 1.0
    coord_col = (2 * grid_col + 1).astype(jnp.float32) / side_float - 1.0
    angles_row = jnp.where(is_patch[:, None], coord_row[:, None] * frequency[None, :], 0.0)
    angles_col = jnp.where(is_patch[:, None], coord_col[:, None] * frequency[None, :], 0.0)

    def rotate_half(block_vals, angles):
        first_half = block_vals[..., :quarter]
        second_half = block_vals[..., quarter:]
        cosine = jnp.cos(angles)[:, None, :]
        sine_part = jnp.sin(angles)[:, None, :]
        return jnp.concatenate(
            [
                first_half * cosine - second_half * sine_part,
                second_half * cosine + first_half * sine_part,
            ],
            axis=-1,
        )

    return jnp.concatenate(
        [
            rotate_half(vectors[..., : 2 * quarter], angles_row),
            rotate_half(vectors[..., 2 * quarter :], angles_col),
        ],
        axis=-1,
    )


def attend_blocks(query_matrix, kv_blocks, key_segment, key_inside, query_segment, query_inside):
    logit_scale_factor = 1.0 / math.sqrt(query_matrix.shape[-1])
    rows_here = query_matrix.shape[0]
    heads_here = query_matrix.shape[1]

    def block_scores(block_of_keys, segment_block, inside_block):
        attention_logits = (
            jnp.einsum(
                "ecn,dcn->ced", query_matrix, block_of_keys, preferred_element_type=jnp.float32
            )
            * logit_scale_factor
        )
        allowed = (
            query_inside[:, None]
            & inside_block[None, :]
            & (query_segment[:, None] == segment_block[None, :])
        )
        return (jnp.where(allowed[None], attention_logits, -1e30), allowed)

    def max_step(carry, input_block_rows):
        row_max, row_total = carry
        masked, allowed = block_scores(
            input_block_rows[0][:, 0], input_block_rows[1], input_block_rows[2]
        )
        new_max = jnp.maximum(row_max, jnp.max(masked, axis=2, keepdims=True))
        exp_terms = jnp.where(allowed[None], jnp.exp(masked - new_max), 0.0)
        row_total = row_total * jnp.exp(row_max - new_max) + jnp.sum(
            exp_terms, axis=2, keepdims=True
        )
        return ((new_max, row_total), None)

    start_max = jnp.full((heads_here, rows_here, 1), -1e30, jnp.float32)
    start_total = jnp.zeros((heads_here, rows_here, 1), jnp.float32)
    (row_max, row_total), _ = lax.scan(
        max_step, (start_max, start_total), (kv_blocks, key_segment, key_inside)
    )
    row_total = jnp.where(query_inside[None, :, None], row_total, 1.0)

    def sum_step(running, input_block_rows):
        masked, allowed = block_scores(
            input_block_rows[0][:, 0], input_block_rows[1], input_block_rows[2]
        )
        exp_terms = jnp.where(allowed[None], jnp.exp(masked - row_max), 0.0)
        softmax_probabilities = (exp_terms / row_total).astype(jnp.bfloat16)
        return (
            running
            + jnp.einsum(
                "vgm,mvb->gvb",
                softmax_probabilities,
                input_block_rows[0][:, 1],
                preferred_element_type=jnp.float32,
            ),
            None,
        )

    start_sum = jnp.zeros((rows_here, heads_here, query_matrix.shape[2]), jnp.float32)
    attended_output, _ = lax.scan(sum_step, start_sum, (kv_blocks, key_segment, key_inside))
    attended_output = jnp.where(query_inside[:, None, None], attended_output, 0.0)
    return attended_output.astype(jnp.bfloat16)


def body(tokens, ln_gain, ln_bias, w_qkv, w_out, layer_scale, grids, offsets):
    rows_here = tokens.shape[0]
    row_count = rows_here * lax.axis_size("seq")
    first_row = lax.axis_index("seq") * rows_here
    gathered = lax.all_gather(tokens, "tp", axis=1, tiled=True)
    widened = gathered.astype(jnp.float32)
    average = jnp.mean(widened, axis=-1, keepdims=True)
    spread_sq = jnp.mean(jnp.square(widened - average), axis=-1, keepdims=True)
    normed = ((widened - average) * lax.rsqrt(spread_sq + 1e-06) * ln_gain + ln_bias).astype(
        jnp.bfloat16
    )
    qkv_sums = jnp.einsum(
        "td,dhcf->thcf",
        normed,
        lax.all_gather(w_qkv, "seq", axis=0, tiled=True),
        preferred_element_type=jnp.float32,
    )
    row_ids = first_row + jnp.arange(rows_here, dtype=jnp.int32)
    segment, inside, is_patch, grid_row, grid_col, grid_side = layout_rows(
        row_ids, offsets, grids, row_count
    )
    query_matrix = rotate(qkv_sums[:, :, 0], is_patch, grid_row, grid_col, grid_side).astype(
        jnp.bfloat16
    )
    roped_keys = rotate(qkv_sums[:, :, 1], is_patch, grid_row, grid_col, grid_side).astype(
        jnp.bfloat16
    )
    values = qkv_sums[:, :, 2].astype(jnp.bfloat16)
    key_value = jnp.stack([roped_keys, values], axis=1)
    block_count = 2 * REACH + 1
    pieces = []
    for block_slot in range(block_count):
        distance = REACH - block_slot
        if distance == 0:
            pieces.append(key_value)
        else:
            pieces.append(from_behind(key_value, "seq", distance))
    kv_blocks = jnp.stack(pieces, axis=0)
    key_rows = first_row - REACH * rows_here + jnp.arange(block_count * rows_here, dtype=jnp.int32)
    key_layout = layout_rows(key_rows, offsets, grids, row_count)
    key_segment = key_layout[0].reshape(block_count, rows_here)
    key_inside = key_layout[1].reshape(block_count, rows_here)
    attended_output = attend_blocks(
        query_matrix, kv_blocks, key_segment, key_inside, segment, inside
    )
    projected = jnp.einsum(
        "thf,hfc->tc",
        attended_output,
        lax.all_gather(w_out, "seq", axis=2, tiled=True),
        preferred_element_type=jnp.float32,
    )
    head_share = lax.psum_scatter(
        projected.astype(jnp.bfloat16), "tp", scatter_dimension=1, tiled=True
    ).astype(jnp.float32)
    layer_out = (tokens.astype(jnp.float32) + layer_scale * head_share).astype(jnp.bfloat16)
    next_rows = from_behind(layer_out[:HALO], "seq", -1)
    extended = jnp.concatenate([layer_out, next_rows], axis=0)
    is_corner = is_patch & (grid_row % 2 == 0) & (grid_col % 2 == 0)
    local_ids = jnp.arange(rows_here, dtype=jnp.int32)
    corner_index = jnp.stack(
        [local_ids, local_ids + 1, local_ids + grid_side, local_ids + grid_side + 1], axis=1
    )
    corner_index = jnp.clip(corner_index, 0, extended.shape[0] - 1)
    merged = jnp.take(extended, corner_index, axis=0)
    return jnp.where(is_corner[:, None, None], merged, jnp.zeros_like(merged))


def solution(mesh):
    placed = (
        P("seq", "tp"),
        P(),
        P(),
        P("seq", "tp", None, None),
        P("tp", None, "seq"),
        P("tp"),
        P(),
        P(),
    )
    return jax.shard_map(
        body, mesh=mesh, in_specs=placed, out_specs=P("seq", None, "tp"), check_vma=False
    )
```

profile of v0, /device:TPU:1, one launch (start us, length us, event | category | flops | bytes accessed | tf_op | source)
XLA Modules:
  0.0 669.1 jit_solution(13033573889273032923)
XLA Ops:
  7.3 1.5 copy.39
  12.0 115.7 %all-gather.4.cloned.1.call-done = bf16[256,4096]{1,0:T(8,128)(2,1)} async-done(((bf16[256,512]{1,0:T(8,128)(2,1)}), bf16[256,4096]{1,0:T(8,128)(2,1)}) %all-gather.4.cloned.1.call-update) | async-done | bytes 2097168 | tf_op jit(solution)/shard_map/all_gather | solution.py:129
  127.7 2.1 convert_reduce_fusion
  129.9 2.3 fusion.24
  132.1 122.1 %all-gather.6.cloned.1.call-done = bf16[4096,2,3,128]{3,0,2,1:T(8,128)(2,1)} async-done(((bf16[64,2,3,128]{3,0,2,1:T(8,128)(2,1)}), bf16[4096,2,3,128]{3,0,2,1:T(8,128)(2,1)}) %all-gather.6.cloned.1.call-update) | async-done | bytes 6291472 | tf_op jit(solution)/shard_map/all_gather | solution.py:139
  254.3 5.7 fusion.29
  260.2 6.1 collective-permute-start
  266.3 2.4 collective-permute-start.1
  268.7 3.8 collective-permute-start.2
  272.5 4.0 collective-permute-start.3
  276.4 3.2 collective-permute-start.4
  279.9 20.5 %collective-permute-start.5 = (bf16[256,2,2,128]{0,3,2,1:T(8,128)(2,1)S(1)}, bf16[256,2,2,128]{0,3,2,1:T(8,128)(2,1)S(1)}, u32[]{:S(2)}, u32[]{:S(2)}) collective-permute-start(bf16[256,2,2,128]{0,3,2,1:T(8,128)(2,1)S(1)} %pad_maximum_fusion.1), channel_id=1, source_target_pairs={{0,16},{8,24},{16,32},{24,40},{32,48},{40,56},{48,64},{56,72},{64,... | collective-permute-start | bytes 786440 | tf_op jit(solution)/shard_map/ppermute | solution.py:14
  301.1 5.2 collective-permute-start.6
  307.1 1.9 collective-permute-start.7
  309.7 1.3 collective-permute-start.8
  311.7 1.3 collective-permute-start.9
  313.7 1.3 collective-permute-start.10
  318.5 22.9 %collective-permute-done.7 = bf16[256,2,2,128]{0,3,2,1:T(8,128)(2,1)S(1)} collective-permute-done((bf16[256,2,2,128]{0,3,2,1:T(8,128)(2,1)S(1)}, bf16[256,2,2,128]{0,3,2,1:T(8,128)(2,1)S(1)}, u32[]{:S(2)}, u32[]{:S(2)}) %collective-permute-start.7) | collective-permute-done | bytes 262176 | tf_op jit(solution)/shard_map/ppermute | solution.py:14
  343.4 3.6 collective-permute-done.8
  349.0 21.4 %collective-permute-done.9 = bf16[256,2,2,128]{0,3,2,1:T(8,128)(2,1)S(1)} collective-permute-done((bf16[256,2,2,128]{0,3,2,1:T(8,128)(2,1)S(1)}, bf16[256,2,2,128]{0,3,2,1:T(8,128)(2,1)S(1)}, u32[]{:S(2)}, u32[]{:S(2)}) %collective-permute-start.9) | collective-permute-done | bytes 262176 | tf_op jit(solution)/shard_map/ppermute | solution.py:14
  371.8 27.3 %collective-permute-done.11 = bf16[256,2,2,128]{0,3,2,1:T(8,128)(2,1)S(1)} collective-permute-done((bf16[256,2,2,128]{0,3,2,1:T(8,128)(2,1)S(1)}, bf16[256,2,2,128]{0,3,2,1:T(8,128)(2,1)S(1)}, u32[]{:S(2)}, u32[]{:S(2)}) %collective-permute-start.11) | collective-permute-done | bytes 262176 | tf_op jit(solution)/shard_map/ppermute | solution.py:14
  399.8 11.2 %collective-permute-done.12 = bf16[256,2,2,128]{0,3,2,1:T(8,128)(2,1)S(1)} collective-permute-done((bf16[256,2,2,128]{0,3,2,1:T(8,128)(2,1)S(1)}, bf16[256,2,2,128]{0,3,2,1:T(8,128)(2,1)S(1)}, u32[]{:S(2)}, u32[]{:S(2)}) %collective-permute-start.12) | collective-permute-done | bytes 262176 | tf_op jit(solution)/shard_map/ppermute | solution.py:14
  411.8 28.7 %collective-permute-done.13 = bf16[256,2,2,128]{0,3,2,1:T(8,128)(2,1)S(1)} collective-permute-done((bf16[256,2,2,128]{0,3,2,1:T(8,128)(2,1)S(1)}, bf16[256,2,2,128]{0,3,2,1:T(8,128)(2,1)S(1)}, u32[]{:S(2)}, u32[]{:S(2)}) %collective-permute-start.13) | collective-permute-done | bytes 262176 | tf_op jit(solution)/shard_map/ppermute | solution.py:14
  441.2 6.3 copy.44
  447.5 24.1 %while.24 = (s32[]{:T(128)}, f32[2,256,1]{1,0,2:T(2,128)S(1)}, f32[2,256,1]{1,0,2:T(2,128)S(1)}, pred[256]{0:T(512)(128)(4,1)S(1)}, pred[15,256]{1,0:T(8,128)(4,...) while((s32[]{:T(128)}, f32[2,256,1]{1,0,2:T(2,128)S(1)}, ...), condition=%wide.region_9.10_spmd.clone, body=%wide.region_6.9_spmd.clone.sunk | while | flops 34540032 | bytes 2063492 | solution.py:97
  471.6 25.9 %while.25 = (s32[]{:T(128)}, f32[256,2,128]{0,2,1:T(8,128)S(1)}, bf16[15,256,2,2,128]{4,1,3,2,0:T(8,128)(2,1)}, pred[256]{0:T(512)(128)(4,1)S(1)}, pred[15,256]{...) while((s32[]{:T(128)}, f32[256,2,128]{0,2,1:T(8,128)S(1)}, ...), condition=%wide.region_11.12_spmd.clone, body=%wide.region_10.11_spmd.clone.sunk | while | flops 68222976 | bytes 1582219 | solution.py:120
  497.5 5.0 all-gather.8.cloned.1.call-done
  502.5 3.7 fusion.21
  506.6 142.4 %reduce-scatter.2.cloned.1.call-done = bf16[256,512]{1,0:T(8,128)(2,1)} async-done(((bf16[256,4096]{1,0:T(8,128)(2,1)}), bf16[256,512]{1,0:T(8,128)(2,1)}) %reduce-scatter.2.cloned.1.call-update) | async-done | bytes 262160 | tf_op jit(solution)/shard_map/reduce_scatter | solution.py:176
  650.1 4.2 collective-permute-start.14
  655.5 4.0 gather_fusion
  659.8 2.8 select_select_fusion
  (297 shorter events, 70.2 us)
Async XLA Ops:
  6.5 247.8 %copy-start.4 = (f32[4096]{0:T(1024)S(1)}, f32[4096]{0:T(1024)}, u32[]{:S(2)}) copy-start(f32[4096]{0:T(1024)} %param.13) | copy-start | bytes 49156
  6.5 247.8 %copy-start.3 = (f32[4096]{0:T(1024)S(1)}, f32[4096]{0:T(1024)}, u32[]{:S(2)}) copy-start(f32[4096]{0:T(1024)} %param.14) | copy-start | bytes 49156
  6.5 121.2 %all-gather.4.cloned.1.call-start = ((), (), s32[]{:S(2)}) async-start(), calls=%async_computation.1 | async-start | bytes 2359296 | tf_op jit(solution)/shard_map/all_gather | solution.py:129
  7.3 247.0 %all-gather.6.cloned.1.call-start = ((), (), s32[]{:S(2)}) async-start(), calls=%async_computation.2 | async-start | bytes 6389760 | tf_op jit(solution)/shard_map/all_gather | solution.py:139
  8.9 493.6 %all-gather.8.cloned.1.call-start = ((), (), s32[]{:S(2)}) async-start(), calls=%async_computation.3 | async-start | bytes 2129920 | tf_op jit(solution)/shard_map/all_gather | solution.py:173
  9.6 639.4 %reduce-scatter.2.cloned.1.call-start = ((), (), s32[]{:S(2)}) async-start(), calls=%async_computation.4 | async-start | bytes 2359296 | tf_op jit(solution)/shard_map/reduce_scatter | solution.py:176
  127.7 126.5 %copy-start = (bf16[256,4096]{1,0:T(8,128)(2,1)S(1)}, bf16[256,4096]{1,0:T(8,128)(2,1)}, u32[]{:S(2)}) copy-start(bf16[256,4096]{1,0:T(8,128)(2,1)} %all-gather.4.cloned.1.call-done) | copy-start | bytes 6291460
  260.2 19.7 %collective-permute-start = (bf16[256,2,2,128]{0,3,2,1:T(8,128)(2,1)S(1)}, bf16[256,2,2,128]{0,3,2,1:T(8,128)(2,1)S(1)}, u32[]{:S(2)}, u32[]{:S(2)}) collective-permute-start(bf16[256,2,2,128]{0,3,2,1:T(8,128)(2,1)S(1)} %pad_maximum_fusion.1), channel_id=1, source_target_pairs={{0,56},{8,64},{16,72},{24,80},{32,88},{40,96},{48,104},{56,112},{6... | collective-permute-start | bytes 786440 | tf_op jit(solution)/shard_map/ppermute | solution.py:14
  266.3 34.8 %collective-permute-start.1 = (bf16[256,2,2,128]{0,3,2,1:T(8,128)(2,1)S(1)}, bf16[256,2,2,128]{0,3,2,1:T(8,128)(2,1)S(1)}, u32[]{:S(2)}, u32[]{:S(2)}) collective-permute-start(bf16[256,2,2,128]{0,3,2,1:T(8,128)(2,1)S(1)} %pad_maximum_fusion.1), channel_id=1, source_target_pairs={{0,48},{8,56},{16,64},{24,72},{32,80},{40,88},{48,96},{56,104},{64... | collective-permute-start | bytes 786440 | tf_op jit(solution)/shard_map/ppermute | solution.py:14
  268.7 38.4 %collective-permute-start.2 = (bf16[256,2,2,128]{0,3,2,1:T(8,128)(2,1)S(1)}, bf16[256,2,2,128]{0,3,2,1:T(8,128)(2,1)S(1)}, u32[]{:S(2)}, u32[]{:S(2)}) collective-permute-start(bf16[256,2,2,128]{0,3,2,1:T(8,128)(2,1)S(1)} %pad_maximum_fusion.1), channel_id=1, source_target_pairs={{0,40},{8,48},{16,56},{24,64},{32,72},{40,80},{48,88},{56,96},{64,... | collective-permute-start | bytes 786440 | tf_op jit(solution)/shard_map/ppermute | solution.py:14
  272.5 37.2 %collective-permute-start.3 = (bf16[256,2,2,128]{0,3,2,1:T(8,128)(2,1)S(1)}, bf16[256,2,2,128]{0,3,2,1:T(8,128)(2,1)S(1)}, u32[]{:S(2)}, u32[]{:S(2)}) collective-permute-start(bf16[256,2,2,128]{0,3,2,1:T(8,128)(2,1)S(1)} %pad_maximum_fusion.1), channel_id=1, source_target_pairs={{0,32},{8,40},{16,48},{24,56},{32,64},{40,72},{48,80},{56,88},{64,... | collective-permute-start | bytes 786440 | tf_op jit(solution)/shard_map/ppermute | solution.py:14
  276.4 35.3 %collective-permute-start.4 = (bf16[256,2,2,128]{0,3,2,1:T(8,128)(2,1)S(1)}, bf16[256,2,2,128]{0,3,2,1:T(8,128)(2,1)S(1)}, u32[]{:S(2)}, u32[]{:S(2)}) collective-permute-start(bf16[256,2,2,128]{0,3,2,1:T(8,128)(2,1)S(1)} %pad_maximum_fusion.1), channel_id=1, source_target_pairs={{0,24},{8,32},{16,40},{24,48},{32,56},{40,64},{48,72},{56,80},{64,... | collective-permute-start | bytes 786440 | tf_op jit(solution)/shard_map/ppermute | solution.py:14
  279.9 33.9 %collective-permute-start.5 = (bf16[256,2,2,128]{0,3,2,1:T(8,128)(2,1)S(1)}, bf16[256,2,2,128]{0,3,2,1:T(8,128)(2,1)S(1)}, u32[]{:S(2)}, u32[]{:S(2)}) collective-permute-start(bf16[256,2,2,128]{0,3,2,1:T(8,128)(2,1)S(1)} %pad_maximum_fusion.1), channel_id=1, source_target_pairs={{0,16},{8,24},{16,32},{24,40},{32,48},{40,56},{48,64},{56,72},{64,... | collective-permute-start | bytes 786440 | tf_op jit(solution)/shard_map/ppermute | solution.py:14
  301.1 14.7 %collective-permute-start.6 = (bf16[256,2,2,128]{0,3,2,1:T(8,128)(2,1)S(1)}, bf16[256,2,2,128]{0,3,2,1:T(8,128)(2,1)S(1)}, u32[]{:S(2)}, u32[]{:S(2)}) collective-permute-start(bf16[256,2,2,128]{0,3,2,1:T(8,128)(2,1)S(1)} %pad_maximum_fusion.1), channel_id=1, source_target_pairs={{0,8},{8,16},{16,24},{24,32},{32,40},{40,48},{48,56},{56,64},{64,7... | collective-permute-start | bytes 786440 | tf_op jit(solution)/shard_map/ppermute | solution.py:14
  307.1 34.3 %collective-permute-start.7 = (bf16[256,2,2,128]{0,3,2,1:T(8,128)(2,1)S(1)}, bf16[256,2,2,128]{0,3,2,1:T(8,128)(2,1)S(1)}, u32[]{:S(2)}, u32[]{:S(2)}) collective-permute-start(bf16[256,2,2,128]{0,3,2,1:T(8,128)(2,1)S(1)} %pad_maximum_fusion.1), channel_id=1, source_target_pairs={{8,0},{16,8},{24,16},{32,24},{40,32},{48,40},{56,48},{64,56},{72,6... | collective-permute-start | bytes 786440 | tf_op jit(solution)/shard_map/ppermute | solution.py:14
  309.7 37.3 %collective-permute-start.8 = (bf16[256,2,2,128]{0,3,2,1:T(8,128)(2,1)S(1)}, bf16[256,2,2,128]{0,3,2,1:T(8,128)(2,1)S(1)}, u32[]{:S(2)}, u32[]{:S(2)}) collective-permute-start(bf16[256,2,2,128]{0,3,2,1:T(8,128)(2,1)S(1)} %pad_maximum_fusion.1), channel_id=1, source_target_pairs={{16,0},{24,8},{32,16},{40,24},{48,32},{56,40},{64,48},{72,56},{80,... | collective-permute-start | bytes 786440 | tf_op jit(solution)/shard_map/ppermute | solution.py:14
  311.7 58.6 %collective-permute-start.9 = (bf16[256,2,2,128]{0,3,2,1:T(8,128)(2,1)S(1)}, bf16[256,2,2,128]{0,3,2,1:T(8,128)(2,1)S(1)}, u32[]{:S(2)}, u32[]{:S(2)}) collective-permute-start(bf16[256,2,2,128]{0,3,2,1:T(8,128)(2,1)S(1)} %pad_maximum_fusion.1), channel_id=1, source_target_pairs={{24,0},{32,8},{40,16},{48,24},{56,32},{64,40},{72,48},{80,56},{88,... | collective-permute-start | bytes 786440 | tf_op jit(solution)/shard_map/ppermute | solution.py:14
  313.7 57.4 %collective-permute-start.10 = (bf16[256,2,2,128]{0,3,2,1:T(8,128)(2,1)S(1)}, bf16[256,2,2,128]{0,3,2,1:T(8,128)(2,1)S(1)}, u32[]{:S(2)}, u32[]{:S(2)}) collective-permute-start(bf16[256,2,2,128]{0,3,2,1:T(8,128)(2,1)S(1)} %pad_maximum_fusion.1), channel_id=1, source_target_pairs={{32,0},{40,8},{48,16},{56,24},{64,32},{72,40},{80,48},{88,56},{96,... | collective-permute-start | bytes 786440 | tf_op jit(solution)/shard_map/ppermute | solution.py:14
  315.8 83.4 %collective-permute-start.11 = (bf16[256,2,2,128]{0,3,2,1:T(8,128)(2,1)S(1)}, bf16[256,2,2,128]{0,3,2,1:T(8,128)(2,1)S(1)}, u32[]{:S(2)}, u32[]{:S(2)}) collective-permute-start(bf16[256,2,2,128]{0,3,2,1:T(8,128)(2,1)S(1)} %pad_maximum_fusion.1), channel_id=1, source_target_pairs={{40,0},{48,8},{56,16},{64,24},{72,32},{80,40},{88,48},{96,56},{104... | collective-permute-start | bytes 786440 | tf_op jit(solution)/shard_map/ppermute | solution.py:14
  341.4 69.7 %collective-permute-start.12 = (bf16[256,2,2,128]{0,3,2,1:T(8,128)(2,1)S(1)}, bf16[256,2,2,128]{0,3,2,1:T(8,128)(2,1)S(1)}, u32[]{:S(2)}, u32[]{:S(2)}) collective-permute-start(bf16[256,2,2,128]{0,3,2,1:T(8,128)(2,1)S(1)} %pad_maximum_fusion.1), channel_id=1, source_target_pairs={{48,0},{56,8},{64,16},{72,24},{80,32},{88,40},{96,48},{104,56},{11... | collective-permute-start | bytes 786440 | tf_op jit(solution)/shard_map/ppermute | solution.py:14
  347.0 93.5 %collective-permute-start.13 = (bf16[256,2,2,128]{0,3,2,1:T(8,128)(2,1)S(1)}, bf16[256,2,2,128]{0,3,2,1:T(8,128)(2,1)S(1)}, u32[]{:S(2)}, u32[]{:S(2)}) collective-permute-start(bf16[256,2,2,128]{0,3,2,1:T(8,128)(2,1)S(1)} %pad_maximum_fusion.1), channel_id=1, source_target_pairs={{56,0},{64,8},{72,16},{80,24},{88,32},{96,40},{104,48},{112,56},{1... | collective-permute-start | bytes 786440 | tf_op jit(solution)/shard_map/ppermute | solution.py:14
  497.5 151.5 %copy-start.1 = (bf16[256,512]{1,0:T(8,128)(2,1)S(1)}, bf16[256,512]{1,0:T(8,128)(2,1)}, u32[]{:S(2)}) copy-start(bf16[256,512]{1,0:T(8,128)(2,1)} %param.12) | copy-start | bytes 786436
  497.5 151.5 %copy-start.2 = (f32[512]{0:T(512)S(1)}, f32[512]{0:T(512)}, u32[]{:S(2)}) copy-start(f32[512]{0:T(512)} %param.17) | copy-start | bytes 6148
  650.1 5.4 collective-permute-start.14
Sparse Core Ops, SparseCore 0:
  10.4 117.3 all-gather.3
  129.9 124.3 all-gather.5
  256.5 246.0 all-gather.7
  507.0 141.9 reduce-scatter.1
where the time goes:
time: 671 us; the launch traced here: 669 us
  waiting for transfers between devices  503 us (75%)
  starting transfers between devices  59.1 us (9%)
  local copies, waits for them, and re-layouts  54.2 us (8%)
  matrix products  21 us (3%)
  other arithmetic  17 us (3%)
  between operations  13.6 us (2%)
    reduce_scatter x1, waiting for transfers between devices, body(): lax.psum_scatter(projected.astype(jnp.bfloat16), 'tp', scatter_dimension=...  142 us
    all_gather x1, waiting for transfers between devices, body(): lax.all_gather(w_qkv, 'seq', axis=0, tiled=True)  122 us
    ppermute x15, waiting for transfers between devices, from_behind(): return lax.ppermute(shard, axis, pairs)  116 us
    all_gather x1, waiting for transfers between devices, body(): gathered = lax.all_gather(tokens, 'tp', axis=1, tiled=True)  116 us
    ppermute x15, starting transfers between devices, from_behind(): return lax.ppermute(shard, axis, pairs)  58.9 us
    squeeze x30, local copies, waits for them, and re-layouts, attend_blocks(): lax.scan(max_step, (start_max, start_total), (kv_blocks, key_segment, key...  29.2 us
    unnamed x27, local copies, waits for them, and re-layouts  17.4 us
  transfers between devices with their start and end apart: 19, of which 11 were waited for; matrix products, arithmetic and copies ran while one was open for 12% of the time, Pallas kernels for 0%

commit v1 on v0

--- a/solution.py
+++ b/solution.py
@@ -126,7 +126,16 @@
     rows_here = tokens.shape[0]
     row_count = rows_here * lax.axis_size("seq")
     first_row = lax.axis_index("seq") * rows_here
-    gathered = lax.all_gather(tokens, "tp", axis=1, tiled=True)
+    remake_slots = lambda my_tile, lane_axis: jnp.concatenate(
+        jax.lax.all_to_all(
+            jnp.stack([my_tile for _ in range(jax.lax.axis_size(lane_axis))]),
+            axis_name=lane_axis,
+            split_axis=0,
+            concat_axis=0,
+        ),
+        axis=1,
+    )
+    gathered = remake_slots(tokens, "tp")
     widened = gathered.astype(jnp.float32)
     average = jnp.mean(widened, axis=-1, keepdims=True)
     spread_sq = jnp.mean(jnp.square(widened - average), axis=-1, keepdims=True)

time: 671 us -> 643 us (0.958)
  waiting for transfers between devices: 503 us -> 453 us
  starting transfers between devices: 59.1 us -> 77.4 us
    all_gather x1 -> x0, waiting for transfers between devices: 116 us -> none  [body(): gathered = lax.all_gather(tokens, 'tp', axis=1, tiled=True)]
    all_to_all x0 -> x1, waiting for transfers between devices: none -> 50 us  [body(): jax.lax.all_to_all(jnp.stack([my_tile for _ in range(jax.lax.axis_size(la...]
    all_to_all x0 -> x1, starting transfers between devices: none -> 18.1 us  [body(): jax.lax.all_to_all(jnp.stack([my_tile for _ in range(jax.lax.axis_size(la...]
    all_gather x1, waiting for transfers between devices: 122 us -> 136 us  [body(): lax.all_gather(w_qkv, 'seq', axis=0, tiled=True)]
    unnamed x27 -> x29, local copies, waits for them, and re-layouts: 17.4 us -> 17.4 us
  transfers between devices with their start and end apart: 19 -> 19, of which waited for: 11 -> 11; matrix products, arithmetic and copies ran while one was open for 12% -> 13% of each run, Pallas kernels for 0% -> 0%
where the time goes in v1:
time: 643 us; the launch traced here: 641 us
  waiting for transfers between devices  453 us (70%)
  starting transfers between devices  77.4 us (12%)
  local copies, waits for them, and re-layouts  58.8 us (9%)
  matrix products  21.3 us (3%)
  other arithmetic  15.3 us (2%)
  between operations  13.6 us (2%)
    reduce_scatter x1, waiting for transfers between devices, body(): lax.psum_scatter(projected.astype(jnp.bfloat16), 'tp', scatter_dimension=...  144 us
    all_gather x1, waiting for transfers between devices, body(): lax.all_gather(w_qkv, 'seq', axis=0, tiled=True)  136 us
    ppermute x15, waiting for transfers between devices, from_behind(): return lax.ppermute(shard, axis, pairs)  118 us
    ppermute x15, starting transfers between devices, from_behind(): return lax.ppermute(shard, axis, pairs)  59.3 us
    all_to_all x1, waiting for transfers between devices, body(): jax.lax.all_to_all(jnp.stack([my_tile for _ in range(jax.lax.axis_size(la...  50 us
    squeeze x30, local copies, waits for them, and re-layouts, attend_blocks(): lax.scan(max_step, (start_max, start_total), (kv_blocks, key_segment, key...  29.3 us
    all_to_all x1, starting transfers between devices, body(): jax.lax.all_to_all(jnp.stack([my_tile for _ in range(jax.lax.axis_size(la...  18.1 us
    unnamed x29, local copies, waits for them, and re-layouts  17.4 us
  transfers between devices with their start and end apart: 19, of which 11 were waited for; matrix products, arithmetic and copies ran while one was open for 13% of the time, Pallas kernels for 0%

profile of v1, /device:TPU:1, one launch (start us, length us, event | category | flops | bytes accessed | tf_op | source)
XLA Modules:
  0.0 641.2 jit_solution(14735615439692431995)
XLA Ops:
  6.5 1.6 copy.66
  8.1 2.5 stack.80
  10.6 18.1 %all-to-all-start = ((bf16[8,256,512]{2,1,0:T(8,128)(2,1)}), bf16[8,256,512]{2,1,0:T(8,128)(2,1)}, u32[]{:S(2)}, u32[]{:S(2)}) async-start(bf16[8,256,512]{2,1,0:T(8,128)(2,1)} %stack.80), calls=%async_computation | async-start | bytes 4194304 | tf_op jit(solution)/shard_map/all_to_all | solution.py:130
  30.5 50.0 %all-to-all-done = bf16[8,256,512]{2,1,0:T(8,128)(2,1)} async-done(((bf16[8,256,512]{2,1,0:T(8,128)(2,1)}), bf16[8,256,512]{2,1,0:T(8,128)(2,1)}, u32[]{:S(2)}, u32[]{:S(2)}) %all-to-all-start) | async-done | bytes 2097184 | tf_op jit(solution)/shard_map/all_to_all | solution.py:130
  80.5 2.8 copy.65
  84.5 2.2 fusion.25
  86.8 136.1 %all-gather.3.cloned.1.call-done = bf16[4096,2,3,128]{3,0,2,1:T(8,128)(2,1)} async-done(((bf16[64,2,3,128]{3,0,2,1:T(8,128)(2,1)}), bf16[4096,2,3,128]{3,0,2,1:T(8,128)(2,1)}) %all-gather.3.cloned.1.call-update) | async-done | bytes 6291472 | tf_op jit(solution)/shard_map/all_gather | solution.py:148
  222.9 6.0 fusion.26
  229.0 6.4 %collective-permute-start = (bf16[256,2,2,128]{0,3,2,1:T(8,128)(2,1)S(1)}, bf16[256,2,2,128]{0,3,2,1:T(8,128)(2,1)S(1)}, u32[]{:S(2)}, u32[]{:S(2)}) collective-permute-start(bf16[256,2,2,128]{0,3,2,1:T(8,128)(2,1)S(1)} %pad_maximum_fusion.1), channel_id=1, source_target_pairs={{0,56},{8,64},{16,72},{24,80},{32,88},{40,96},{48,104},{56,112},{6... | collective-permute-start | bytes 786440 | tf_op jit(solution)/shard_map/ppermute | solution.py:14
  235.4 3.0 collective-permute-start.1
  238.5 5.3 collective-permute-start.2
  243.8 6.3 collective-permute-start.3
  250.1 1.3 collective-permute-start.4
  251.6 18.0 %collective-permute-start.5 = (bf16[256,2,2,128]{0,3,2,1:T(8,128)(2,1)S(1)}, bf16[256,2,2,128]{0,3,2,1:T(8,128)(2,1)S(1)}, u32[]{:S(2)}, u32[]{:S(2)}) collective-permute-start(bf16[256,2,2,128]{0,3,2,1:T(8,128)(2,1)S(1)} %pad_maximum_fusion.1), channel_id=1, source_target_pairs={{0,16},{8,24},{16,32},{24,40},{32,48},{40,56},{48,64},{56,72},{64,... | collective-permute-start | bytes 786440 | tf_op jit(solution)/shard_map/ppermute | solution.py:14
  270.3 5.2 collective-permute-start.6
  276.3 1.9 collective-permute-start.7
  278.9 1.3 collective-permute-start.8
  287.7 9.0 %collective-permute-done.7 = bf16[256,2,2,128]{0,3,2,1:T(8,128)(2,1)S(1)} collective-permute-done((bf16[256,2,2,128]{0,3,2,1:T(8,128)(2,1)S(1)}, bf16[256,2,2,128]{0,3,2,1:T(8,128)(2,1)S(1)}, u32[]{:S(2)}, u32[]{:S(2)}) %collective-permute-start.7) | collective-permute-done | bytes 262176 | tf_op jit(solution)/shard_map/ppermute | solution.py:14
  298.7 19.1 %collective-permute-done.8 = bf16[256,2,2,128]{0,3,2,1:T(8,128)(2,1)S(1)} collective-permute-done((bf16[256,2,2,128]{0,3,2,1:T(8,128)(2,1)S(1)}, bf16[256,2,2,128]{0,3,2,1:T(8,128)(2,1)S(1)}, u32[]{:S(2)}, u32[]{:S(2)}) %collective-permute-start.8) | collective-permute-done | bytes 262176 | tf_op jit(solution)/shard_map/ppermute | solution.py:14
  319.8 21.4 %collective-permute-done.9 = bf16[256,2,2,128]{0,3,2,1:T(8,128)(2,1)S(1)} collective-permute-done((bf16[256,2,2,128]{0,3,2,1:T(8,128)(2,1)S(1)}, bf16[256,2,2,128]{0,3,2,1:T(8,128)(2,1)S(1)}, u32[]{:S(2)}, u32[]{:S(2)}) %collective-permute-start.9) | collective-permute-done | bytes 262176 | tf_op jit(solution)/shard_map/ppermute | solution.py:14
  342.7 27.1 %collective-permute-done.11 = bf16[256,2,2,128]{0,3,2,1:T(8,128)(2,1)S(1)} collective-permute-done((bf16[256,2,2,128]{0,3,2,1:T(8,128)(2,1)S(1)}, bf16[256,2,2,128]{0,3,2,1:T(8,128)(2,1)S(1)}, u32[]{:S(2)}, u32[]{:S(2)}) %collective-permute-start.11) | collective-permute-done | bytes 262176 | tf_op jit(solution)/shard_map/ppermute | solution.py:14
  370.5 11.1 %collective-permute-done.12 = bf16[256,2,2,128]{0,3,2,1:T(8,128)(2,1)S(1)} collective-permute-done((bf16[256,2,2,128]{0,3,2,1:T(8,128)(2,1)S(1)}, bf16[256,2,2,128]{0,3,2,1:T(8,128)(2,1)S(1)}, u32[]{:S(2)}, u32[]{:S(2)}) %collective-permute-start.12) | collective-permute-done | bytes 262176 | tf_op jit(solution)/shard_map/ppermute | solution.py:14
  382.3 29.0 %collective-permute-done.13 = bf16[256,2,2,128]{0,3,2,1:T(8,128)(2,1)S(1)} collective-permute-done((bf16[256,2,2,128]{0,3,2,1:T(8,128)(2,1)S(1)}, bf16[256,2,2,128]{0,3,2,1:T(8,128)(2,1)S(1)}, u32[]{:S(2)}, u32[]{:S(2)}) %collective-permute-start.13) | collective-permute-done | bytes 262176 | tf_op jit(solution)/shard_map/ppermute | solution.py:14
  412.1 6.3 copy.72
  418.3 24.1 %while.24 = (s32[]{:T(128)}, f32[2,256,1]{1,0,2:T(2,128)S(1)}, f32[2,256,1]{1,0,2:T(2,128)S(1)}, pred[256]{0:T(512)(128)(4,1)S(1)}, pred[15,256]{1,0:T(8,128)(4,...) while((s32[]{:T(128)}, f32[2,256,1]{1,0,2:T(2,128)S(1)}, ...), condition=%wide.region_9.10_spmd.clone, body=%wide.region_6.9_spmd.clone.sunk | while | flops 34540032 | bytes 2063492 | solution.py:97
  442.5 25.9 %while.25 = (s32[]{:T(128)}, f32[256,2,128]{0,2,1:T(8,128)S(1)}, bf16[15,256,2,2,128]{4,1,3,2,0:T(8,128)(2,1)}, pred[256]{0:T(512)(128)(4,1)S(1)}, pred[15,256]{...) while((s32[]{:T(128)}, f32[256,2,128]{0,2,1:T(8,128)S(1)}, ...), condition=%wide.region_11.12_spmd.clone, body=%wide.region_10.11_spmd.clone.sunk | while | flops 68222976 | bytes 1582219 | solution.py:120
  468.4 4.9 all-gather.5.cloned.1.call-done
  473.3 3.7 fusion.21
  477.4 143.7 %reduce-scatter.2.cloned.1.call-done = bf16[256,512]{1,0:T(8,128)(2,1)} async-done(((bf16[256,4096]{1,0:T(8,128)(2,1)}), bf16[256,512]{1,0:T(8,128)(2,1)}) %reduce-scatter.2.cloned.1.call-update) | async-done | bytes 262160 | tf_op jit(solution)/shard_map/reduce_scatter | solution.py:185
  622.1 4.1 collective-permute-start.14
  627.6 4.0 gather_fusion
  631.8 2.8 select_select_fusion
  (301 shorter events, 71.8 us)
Async XLA Ops:
  6.5 23.0 %copy-start.4 = (s32[15]{0:T(128)S(1)}, s32[15]{0:T(128)}, u32[]{:S(2)}) copy-start(s32[15]{0:T(128)} %param.19) | copy-start | bytes 184
  6.5 23.3 %copy-start.5 = (s32[14]{0:T(128)S(1)}, s32[14]{0:T(128)}, u32[]{:S(2)}) copy-start(s32[14]{0:T(128)} %param.18) | copy-start | bytes 172
  6.5 216.3 %all-gather.3.cloned.1.call-start = ((), (), s32[]{:S(2)}) async-start(), calls=%async_computation.2 | async-start | bytes 6389760 | tf_op jit(solution)/shard_map/all_gather | solution.py:148
  10.6 69.9 %all-to-all-start = ((bf16[8,256,512]{2,1,0:T(8,128)(2,1)}), bf16[8,256,512]{2,1,0:T(8,128)(2,1)}, u32[]{:S(2)}, u32[]{:S(2)}) async-start(bf16[8,256,512]{2,1,0:T(8,128)(2,1)} %stack.80), calls=%async_computation | async-start | bytes 4194304 | tf_op jit(solution)/shard_map/all_to_all | solution.py:130
  28.7 444.6 %all-gather.5.cloned.1.call-start = ((), (), s32[]{:S(2)}) async-start(), calls=%async_computation.3 | async-start | bytes 2129920 | tf_op jit(solution)/shard_map/all_gather | solution.py:182
  29.4 591.6 %reduce-scatter.2.cloned.1.call-start = ((), (), s32[]{:S(2)}) async-start(), calls=%async_computation.4 | async-start | bytes 2359296 | tf_op jit(solution)/shard_map/reduce_scatter | solution.py:185
  30.5 54.1 %copy-start.1 = (f32[4096]{0:T(1024)S(1)}, f32[4096]{0:T(1024)}, u32[]{:S(2)}) copy-start(f32[4096]{0:T(1024)} %param.14) | copy-start | bytes 49156
  30.5 54.1 %copy-start.2 = (f32[4096]{0:T(1024)S(1)}, f32[4096]{0:T(1024)}, u32[]{:S(2)}) copy-start(f32[4096]{0:T(1024)} %param.13) | copy-start | bytes 49156
  229.0 22.6 %collective-permute-start = (bf16[256,2,2,128]{0,3,2,1:T(8,128)(2,1)S(1)}, bf16[256,2,2,128]{0,3,2,1:T(8,128)(2,1)S(1)}, u32[]{:S(2)}, u32[]{:S(2)}) collective-permute-start(bf16[256,2,2,128]{0,3,2,1:T(8,128)(2,1)S(1)} %pad_maximum_fusion.1), channel_id=1, source_target_pairs={{0,56},{8,64},{16,72},{24,80},{32,88},{40,96},{48,104},{56,112},{6... | collective-permute-start | bytes 786440 | tf_op jit(solution)/shard_map/ppermute | solution.py:14
  235.4 34.9 %collective-permute-start.1 = (bf16[256,2,2,128]{0,3,2,1:T(8,128)(2,1)S(1)}, bf16[256,2,2,128]{0,3,2,1:T(8,128)(2,1)S(1)}, u32[]{:S(2)}, u32[]{:S(2)}) collective-permute-start(bf16[256,2,2,128]{0,3,2,1:T(8,128)(2,1)S(1)} %pad_maximum_fusion.1), channel_id=1, source_target_pairs={{0,48},{8,56},{16,64},{24,72},{32,80},{40,88},{48,96},{56,104},{64... | collective-permute-start | bytes 786440 | tf_op jit(solution)/shard_map/ppermute | solution.py:14
  238.5 37.8 %collective-permute-start.2 = (bf16[256,2,2,128]{0,3,2,1:T(8,128)(2,1)S(1)}, bf16[256,2,2,128]{0,3,2,1:T(8,128)(2,1)S(1)}, u32[]{:S(2)}, u32[]{:S(2)}) collective-permute-start(bf16[256,2,2,128]{0,3,2,1:T(8,128)(2,1)S(1)} %pad_maximum_fusion.1), channel_id=1, source_target_pairs={{0,40},{8,48},{16,56},{24,64},{32,72},{40,80},{48,88},{56,96},{64,... | collective-permute-start | bytes 786440 | tf_op jit(solution)/shard_map/ppermute | solution.py:14
  243.8 35.1 %collective-permute-start.3 = (bf16[256,2,2,128]{0,3,2,1:T(8,128)(2,1)S(1)}, bf16[256,2,2,128]{0,3,2,1:T(8,128)(2,1)S(1)}, u32[]{:S(2)}, u32[]{:S(2)}) collective-permute-start(bf16[256,2,2,128]{0,3,2,1:T(8,128)(2,1)S(1)} %pad_maximum_fusion.1), channel_id=1, source_target_pairs={{0,32},{8,40},{16,48},{24,56},{32,64},{40,72},{48,80},{56,88},{64,... | collective-permute-start | bytes 786440 | tf_op jit(solution)/shard_map/ppermute | solution.py:14
  250.1 30.8 %collective-permute-start.4 = (bf16[256,2,2,128]{0,3,2,1:T(8,128)(2,1)S(1)}, bf16[256,2,2,128]{0,3,2,1:T(8,128)(2,1)S(1)}, u32[]{:S(2)}, u32[]{:S(2)}) collective-permute-start(bf16[256,2,2,128]{0,3,2,1:T(8,128)(2,1)S(1)} %pad_maximum_fusion.1), channel_id=1, source_target_pairs={{0,24},{8,32},{16,40},{24,48},{32,56},{40,64},{48,72},{56,80},{64,... | collective-permute-start | bytes 786440 | tf_op jit(solution)/shard_map/ppermute | solution.py:14
  251.6 31.3 %collective-permute-start.5 = (bf16[256,2,2,128]{0,3,2,1:T(8,128)(2,1)S(1)}, bf16[256,2,2,128]{0,3,2,1:T(8,128)(2,1)S(1)}, u32[]{:S(2)}, u32[]{:S(2)}) collective-permute-start(bf16[256,2,2,128]{0,3,2,1:T(8,128)(2,1)S(1)} %pad_maximum_fusion.1), channel_id=1, source_target_pairs={{0,16},{8,24},{16,32},{24,40},{32,48},{40,56},{48,64},{56,72},{64,... | collective-permute-start | bytes 786440 | tf_op jit(solution)/shard_map/ppermute | solution.py:14
  270.3 14.6 %collective-permute-start.6 = (bf16[256,2,2,128]{0,3,2,1:T(8,128)(2,1)S(1)}, bf16[256,2,2,128]{0,3,2,1:T(8,128)(2,1)S(1)}, u32[]{:S(2)}, u32[]{:S(2)}) collective-permute-start(bf16[256,2,2,128]{0,3,2,1:T(8,128)(2,1)S(1)} %pad_maximum_fusion.1), channel_id=1, source_target_pairs={{0,8},{8,16},{16,24},{24,32},{32,40},{40,48},{48,56},{56,64},{64,7... | collective-permute-start | bytes 786440 | tf_op jit(solution)/shard_map/ppermute | solution.py:14
  276.3 20.4 %collective-permute-start.7 = (bf16[256,2,2,128]{0,3,2,1:T(8,128)(2,1)S(1)}, bf16[256,2,2,128]{0,3,2,1:T(8,128)(2,1)S(1)}, u32[]{:S(2)}, u32[]{:S(2)}) collective-permute-start(bf16[256,2,2,128]{0,3,2,1:T(8,128)(2,1)S(1)} %pad_maximum_fusion.1), channel_id=1, source_target_pairs={{8,0},{16,8},{24,16},{32,24},{40,32},{48,40},{56,48},{64,56},{72,6... | collective-permute-start | bytes 786440 | tf_op jit(solution)/shard_map/ppermute | solution.py:14
  278.9 38.9 %collective-permute-start.8 = (bf16[256,2,2,128]{0,3,2,1:T(8,128)(2,1)S(1)}, bf16[256,2,2,128]{0,3,2,1:T(8,128)(2,1)S(1)}, u32[]{:S(2)}, u32[]{:S(2)}) collective-permute-start(bf16[256,2,2,128]{0,3,2,1:T(8,128)(2,1)S(1)} %pad_maximum_fusion.1), channel_id=1, source_target_pairs={{16,0},{24,8},{32,16},{40,24},{48,32},{56,40},{64,48},{72,56},{80,... | collective-permute-start | bytes 786440 | tf_op jit(solution)/shard_map/ppermute | solution.py:14
  280.9 60.3 %collective-permute-start.9 = (bf16[256,2,2,128]{0,3,2,1:T(8,128)(2,1)S(1)}, bf16[256,2,2,128]{0,3,2,1:T(8,128)(2,1)S(1)}, u32[]{:S(2)}, u32[]{:S(2)}) collective-permute-start(bf16[256,2,2,128]{0,3,2,1:T(8,128)(2,1)S(1)} %pad_maximum_fusion.1), channel_id=1, source_target_pairs={{24,0},{32,8},{40,16},{48,24},{56,32},{64,40},{72,48},{80,56},{88,... | collective-permute-start | bytes 786440 | tf_op jit(solution)/shard_map/ppermute | solution.py:14
  282.9 59.0 %collective-permute-start.10 = (bf16[256,2,2,128]{0,3,2,1:T(8,128)(2,1)S(1)}, bf16[256,2,2,128]{0,3,2,1:T(8,128)(2,1)S(1)}, u32[]{:S(2)}, u32[]{:S(2)}) collective-permute-start(bf16[256,2,2,128]{0,3,2,1:T(8,128)(2,1)S(1)} %pad_maximum_fusion.1), channel_id=1, source_target_pairs={{32,0},{40,8},{48,16},{56,24},{64,32},{72,40},{80,48},{88,56},{96,... | collective-permute-start | bytes 786440 | tf_op jit(solution)/shard_map/ppermute | solution.py:14
  285.0 84.8 %collective-permute-start.11 = (bf16[256,2,2,128]{0,3,2,1:T(8,128)(2,1)S(1)}, bf16[256,2,2,128]{0,3,2,1:T(8,128)(2,1)S(1)}, u32[]{:S(2)}, u32[]{:S(2)}) collective-permute-start(bf16[256,2,2,128]{0,3,2,1:T(8,128)(2,1)S(1)} %pad_maximum_fusion.1), channel_id=1, source_target_pairs={{40,0},{48,8},{56,16},{64,24},{72,32},{80,40},{88,48},{96,56},{104... | collective-permute-start | bytes 786440 | tf_op jit(solution)/shard_map/ppermute | solution.py:14
  296.7 84.9 %collective-permute-start.12 = (bf16[256,2,2,128]{0,3,2,1:T(8,128)(2,1)S(1)}, bf16[256,2,2,128]{0,3,2,1:T(8,128)(2,1)S(1)}, u32[]{:S(2)}, u32[]{:S(2)}) collective-permute-start(bf16[256,2,2,128]{0,3,2,1:T(8,128)(2,1)S(1)} %pad_maximum_fusion.1), channel_id=1, source_target_pairs={{48,0},{56,8},{64,16},{72,24},{80,32},{88,40},{96,48},{104,56},{11... | collective-permute-start | bytes 786440 | tf_op jit(solution)/shard_map/ppermute | solution.py:14
  317.8 93.5 %collective-permute-start.13 = (bf16[256,2,2,128]{0,3,2,1:T(8,128)(2,1)S(1)}, bf16[256,2,2,128]{0,3,2,1:T(8,128)(2,1)S(1)}, u32[]{:S(2)}, u32[]{:S(2)}) collective-permute-start(bf16[256,2,2,128]{0,3,2,1:T(8,128)(2,1)S(1)} %pad_maximum_fusion.1), channel_id=1, source_target_pairs={{56,0},{64,8},{72,16},{80,24},{88,32},{96,40},{104,48},{112,56},{1... | collective-permute-start | bytes 786440 | tf_op jit(solution)/shard_map/ppermute | solution.py:14
  468.4 152.7 %copy-start = (bf16[256,512]{1,0:T(8,128)(2,1)S(1)}, bf16[256,512]{1,0:T(8,128)(2,1)}, u32[]{:S(2)}) copy-start(bf16[256,512]{1,0:T(8,128)(2,1)} %param.12) | copy-start | bytes 786436
  468.4 152.7 %copy-start.3 = (f32[512]{0:T(512)S(1)}, f32[512]{0:T(512)}, u32[]{:S(2)}) copy-start(f32[512]{0:T(512)} %param.17) | copy-start | bytes 6148
  622.1 5.4 collective-permute-start.14
Sparse Core Ops, SparseCore 0:
  9.5 213.3 all-gather.2
  225.0 248.2 all-gather.4
  478.0 143.0 reduce-scatter.1
